TPU v7x, 128 devices: a whole 4x4x4 slice. The times are simulated.
128 devices in a mesh: rows: 32 (over x, y, core), dims: 4 (over z).
Axes of the slice: x: 4, y: 4, z: 4, core: 2. Of those that a mesh axis runs over, the one named last changes fastest.
Arguments:
- gradients: float32 [65536, 4096], P('rows', 'dims'), may hold values from -0.5 to 0.5
- ridge: float32 [], replicated, may hold values from 2 to 8
- panel_index: int32 [1], replicated, may hold values from 0 to 63
- block_ids: int32 [64], replicated, may hold values from 0 to 63, each once
Outputs:
- panel: float32 [65536, 1024], P(('rows', 'dims'))
Inputs may be any that keep to these rules, and one draw needn't show every extreme that they name: block_ids is a permutation of the row blocks' numbers.
All inputs are finite; a program needn't handle non-finite values.
Results may differ from a plain program's by a relative error of at most 0.000081.
Values sent between devices are 32-bit elements; how exact they have to be, the bound alone decides.
No kernel may reach another device: no remote copies, remote signals or barrier semaphores. Data moves between devices by JAX's collectives and lax.ppermute only.
A program may use at most 128 MiB of HBM per device.

v0:
```python
import jax
import jax.numpy as jnp
from jax import lax
from jax.sharding import PartitionSpec as P

B = 1024


def broadcast(array, axis, root):
    mine = lax.axis_index(axis) == root
    return lax.psum(jnp.where(mine, array, jnp.zeros_like(array)), axis)


def per_device(gradients, ridge, panel_index, block_ids):
    local_rows = gradients.shape[0]
    blocks_here = local_rows // B
    ids = jnp.arange(block_ids.shape[0], dtype=jnp.int32)
    position = jnp.sum(jnp.where(block_ids == panel_index[0], ids, 0))
    owner = position // blocks_here
    offset = position % blocks_here * B
    own_tile = lax.dynamic_slice_in_dim(gradients, offset, B, 0)
    pivot = broadcast(own_tile, "rows", owner)
    numbers = (((1,), (1,)), ((), ()))
    share = local_rows // lax.axis_size("dims")
    tile_term = lax.dot_general(
        pivot, pivot, numbers, precision=lax.Precision.HIGHEST, preferred_element_type=jnp.float32
    )
    summed, tile = lax.psum(
        (
            lax.dot_general(
                gradients,
                pivot,
                numbers,
                precision=lax.Precision.HIGHEST,
                preferred_element_type=jnp.float32,
            ),
            tile_term,
        ),
        "dims",
    )
    column = lax.dynamic_slice_in_dim(summed, lax.axis_index("dims") * share, share, 0)
    first = lax.axis_index("rows") * local_rows + lax.axis_index("dims") * share
    row_ids = first + jnp.arange(share, dtype=jnp.int32)[:, None]
    col_ids = position * B + jnp.arange(B, dtype=jnp.int32)[None, :]
    column = column + jnp.where(row_ids == col_ids, ridge, jnp.float32(0.0))
    factor = jnp.linalg.cholesky(tile + ridge * jnp.eye(B, dtype=jnp.float32))
    return lax.linalg.triangular_solve(
        factor, column, left_side=False, lower=True, transpose_a=True
    )


def solution(mesh):
    in_specs = (P("rows", "dims"), P(), P(), P())
    out_specs = P(("rows", "dims"), None)
    return jax.shard_map(
        per_device, mesh=mesh, in_specs=in_specs, out_specs=out_specs, check_vma=False
    )
```

profile of v0, /device:TPU:1, one launch (start us, length us, event | category | flops | bytes accessed | tf_op | source)
XLA Modules:
  0.0 797.1 jit_solution(7340139209575436827)
XLA Ops:
  11.0 4.7 constant_dynamic-slice_fusion.1
  15.7 5.3 copy.33
  21.1 2.8 broadcast_select_fusion
  23.9 114.7 %all-reduce.5.cloned.1.call-done = f32[1024,1024]{0,1:T(8,128)} async-done(((f32[1024,1024]{0,1:T(8,128)}), f32[1024,1024]{0,1:T(8,128)}) %all-reduce.5.cloned.1.call-update) | async-done | bytes 4194320 | tf_op jit(solution)/shard_map/psum | solution.py:11
  138.7 57.2 %convolution_bitcast_fusion = f32[2048,1024]{0,1:T(8,128)} fusion(f32[1024,1024]{0,1:T(8,128)} %all-reduce.5.cloned.1.call-done, f32[2048,1024]{1,0:T(8,128)} %param.4), kind=kOutput, calls=%fused_computation.3 | convolution fusion | flops 25769803776 | bytes 20971520 | tf_op jit(solution)/shard_map/dot_general | solution.py:30
  195.9 15.0 %fusion.63 = f32[1024,1024]{0,1:T(8,128)} fusion(f32[1024,1024]{0,1:T(8,128)S(1)} %copy-done.2), kind=kOutput, calls=%fused_computation.165 | convolution fusion | flops 12884901888 | bytes 8388608 | tf_op jit(solution)/shard_map/dot_general | solution.py:25
  212.2 226.6 %all-reduce.7.cloned.1.call-done = (f32[2048,1024]{0,1:T(8,128)}, f32[1024,1024]{0,1:T(8,128)}) async-done(((f32[2048,1024]{0,1:T(8,128)}, f32[1024,1024]{0,1:T(8,128)}), (f32[2048,1024]{0,1:T(8,128)}, f32[1024,1024]{0,1:T(8,128)})) %all-reduce.7.cloned.1.call-update) | async-done | bytes 12582928 | tf_op jit(solution)/shard_map/psum | solution.py:28
  438.8 4.8 select_add_fusion
  443.6 5.7 copy.7
  449.4 4.5 fusion
  455.8 11.7 %cholesky.222 = f32[128,128]{1,0:T(8,128)S(1)} custom-call(f32[128,128]{1,0:T(8,128)S(1)} %cholesky.577), custom_call_target="Cholesky" | custom-call | tf_op jit(solution)/shard_map/jit(cholesky)/cholesky | solution.py:46
  467.6 9.8 %custom-call.62 = f32[1,128,128]{1,2,0:T(8,128)S(1)} custom-call(f32[1,128,128]{2,1,0:T(8,128)S(1)} %get-tuple-element.67), custom_call_target="InvertDiagBlocksLowerTriangular" | custom-call | tf_op jit(solution)/shard_map/jit(cholesky)/cholesky | solution.py:46
  480.5 11.7 %cholesky.243 = f32[128,128]{1,0:T(8,128)S(1)} custom-call(f32[128,128]{1,0:T(8,128)S(1)} %cholesky.581), custom_call_target="Cholesky" | custom-call | tf_op jit(solution)/shard_map/jit(cholesky)/cholesky | solution.py:46
  492.8 9.8 %custom-call.63 = f32[1,128,128]{1,2,0:T(8,128)S(1)} custom-call(f32[1,128,128]{2,1,0:T(8,128)S(1)} %get-tuple-element.65), custom_call_target="InvertDiagBlocksLowerTriangular" | custom-call | tf_op jit(solution)/shard_map/jit(cholesky)/cholesky | solution.py:46
  508.1 11.7 %cholesky.466 = f32[128,128]{1,0:T(8,128)S(1)} custom-call(f32[128,128]{1,0:T(8,128)S(1)} %cholesky.586), custom_call_target="Cholesky" | custom-call | tf_op jit(solution)/shard_map/jit(cholesky)/cholesky | solution.py:46
  520.6 9.8 %custom-call.64 = f32[1,128,128]{1,2,0:T(8,128)S(1)} custom-call(f32[1,128,128]{2,1,0:T(8,128)S(1)} %get-tuple-element.63), custom_call_target="InvertDiagBlocksLowerTriangular" | custom-call | tf_op jit(solution)/shard_map/jit(cholesky)/cholesky | solution.py:46
  531.7 3.3 convolution_subtract_fusion.2
  535.0 11.7 %cholesky.485 = f32[128,128]{1,0:T(8,128)S(1)} custom-call(f32[128,128]{1,0:T(8,128)S(1)} %cholesky.591), custom_call_target="Cholesky" | custom-call | tf_op jit(solution)/shard_map/jit(cholesky)/cholesky | solution.py:46
  547.5 9.8 %custom-call.65 = f32[1,128,128]{1,2,0:T(8,128)S(1)} custom-call(f32[1,128,128]{2,1,0:T(8,128)S(1)} %get-tuple-element.61), custom_call_target="InvertDiagBlocksLowerTriangular" | custom-call | tf_op jit(solution)/shard_map/jit(cholesky)/cholesky | solution.py:46
  558.5 3.2 convolution_subtract_fusion.10
  561.6 12.1 %cholesky.504 = f32[128,128]{1,0:T(8,128)S(1)} custom-call(f32[128,128]{1,0:T(8,128)S(1)} %cholesky.596), custom_call_target="Cholesky" | custom-call | tf_op jit(solution)/shard_map/jit(cholesky)/cholesky | solution.py:46
  574.5 9.8 %custom-call.66 = f32[1,128,128]{1,2,0:T(8,128)S(1)} custom-call(f32[1,128,128]{2,1,0:T(8,128)S(1)} %get-tuple-element.59), custom_call_target="InvertDiagBlocksLowerTriangular" | custom-call | tf_op jit(solution)/shard_map/jit(cholesky)/cholesky | solution.py:46
  585.4 3.1 convolution_subtract_fusion.11
  588.5 11.7 %cholesky.524 = f32[128,128]{1,0:T(8,128)S(1)} custom-call(f32[128,128]{1,0:T(8,128)S(1)} %cholesky.601), custom_call_target="Cholesky" | custom-call | tf_op jit(solution)/shard_map/jit(cholesky)/cholesky | solution.py:46
  601.0 9.8 %custom-call.67 = f32[1,128,128]{1,2,0:T(8,128)S(1)} custom-call(f32[1,128,128]{2,1,0:T(8,128)S(1)} %get-tuple-element.57), custom_call_target="InvertDiagBlocksLowerTriangular" | custom-call | tf_op jit(solution)/shard_map/jit(cholesky)/cholesky | solution.py:46
  611.8 2.8 convolution_subtract_fusion.12
  614.7 11.7 %cholesky.544 = f32[128,128]{1,0:T(8,128)S(1)} custom-call(f32[128,128]{1,0:T(8,128)S(1)} %cholesky.606), custom_call_target="Cholesky" | custom-call | tf_op jit(solution)/shard_map/jit(cholesky)/cholesky | solution.py:46
  627.2 9.8 %custom-call.68 = f32[1,128,128]{1,2,0:T(8,128)S(1)} custom-call(f32[1,128,128]{2,1,0:T(8,128)S(1)} %get-tuple-element.55), custom_call_target="InvertDiagBlocksLowerTriangular" | custom-call | tf_op jit(solution)/shard_map/jit(cholesky)/cholesky | solution.py:46
  640.0 11.7 %cholesky.562 = f32[128,128]{1,0:T(8,128)S(1)} custom-call(f32[128,128]{1,0:T(8,128)S(1)} %convolution_subtract_fusion.13), custom_call_target="Cholesky" | custom-call | tf_op jit(solution)/shard_map/jit(cholesky)/cholesky | solution.py:46
  661.9 4.9 select_select_fusion
  666.8 24.5 %while.1 = (s32[]{:T(128)}, f32[1024,1024]{0,1:T(8,128)}, s32[8,2]{0,1:T(2,128)S(1)}, f32[8,128,128]{2,1,0:T(8,128)S(1)}, s32[]{:T(128)}) while((s32[]{:T(128)}, f32[1024,1024]{0,1:T(8,128)}, s32[8,2]{0,1:T(2,128)S(1)}, f32[8,128,128]{2,1,0:T(8,128)S(1)}, s32[]{:T(128)}) %tuple.50), condition=%wide.while_cond, body=%wide.while_body.sunk | while | flops 2 | bytes 393321 | solution.py:47
  691.3 78.8 %custom-call.69 = f32[8,128,128]{1,2,0:T(8,128)S(1)} custom-call(f32[8,128,128]{2,1,0:T(8,128)S(1)} %get-tuple-element.12), custom_call_target="InvertDiagBlocksLowerTriangular" | custom-call | tf_op jit(solution)/shard_map/triangular_solve | solution.py:47
  (123 shorter events, 73.1 us)
Async XLA Ops:
  6.5 132.1 %all-reduce.5.cloned.1.call-start = ((), (), s32[]{:S(2)}) async-start(), calls=%async_computation | async-start | bytes 8388608 | tf_op jit(solution)/shard_map/psum | solution.py:11
  23.9 414.9 %all-reduce.7.cloned.1.call-start = ((), (), s32[]{:S(2)}) async-start(), calls=%async_computation.1 | async-start | bytes 25165824 | tf_op jit(solution)/shard_map/psum | solution.py:28
  138.7 57.2 %copy-start.2 = (f32[1024,1024]{0,1:T(8,128)S(1)}, f32[1024,1024]{0,1:T(8,128)}, u32[]{:S(2)}) copy-start(f32[1024,1024]{0,1:T(8,128)} %all-reduce.5.cloned.1.call-done) | copy-start | bytes 12582916
  453.8 2.0 copy-start.1
  503.7 2.0 copy-start
Sparse Core Ops, SparseCore 0:
  24.0 114.6 all-reduce.4
  211.0 227.7 all-reduce.6
where the time goes:
time: 808 us; the launch traced here: 797 us
  waiting for transfers between devices  341 us (42%)
  other arithmetic  266 us (33%)
  matrix products  114 us (14%)
  local copies, waits for them, and re-layouts  51.3 us (6%)
  between operations  23.6 us (3%)
    psum x1, waiting for transfers between devices, per_device(): lax.psum((lax.dot_general(gradients, pivot, numbers, precision=lax.Precis...  227 us
    another operation x30, other arithmetic, per_device(): factor = jnp.linalg.cholesky(tile + ridge * jnp.eye(B, dtype=jnp.float32))  168 us
    psum x1, waiting for transfers between devices, broadcast(): return lax.psum(jnp.where(mine, array, jnp.zeros_like(array)), axis)  115 us
    another operation x3, other arithmetic, per_device(): lax.linalg.triangular_solve(factor, column, left_side=False, lower=True,...  83.7 us
    dot_general x1, matrix products, per_device(): lax.dot_general(gradients, pivot, numbers, precision=lax.Precision.HIGHES...  57.2 us
    another operation x14, matrix products, per_device(): factor = jnp.linalg.cholesky(tile + ridge * jnp.eye(B, dtype=jnp.float32))  25.9 us
    another operation x40, local copies, waits for them, and re-layouts  24.2 us
  transfers between devices with their start and end apart: 2, of which 2 were waited for; matrix products, arithmetic and copies ran while one was open for 0% of the time, Pallas kernels for 0%

commit v1 on v0

--- a/solution.py
+++ b/solution.py
@@ -22,23 +22,36 @@
     pivot = broadcast(own_tile, "rows", owner)
     numbers = (((1,), (1,)), ((), ()))
     share = local_rows // lax.axis_size("dims")
-    tile_term = lax.dot_general(
-        pivot, pivot, numbers, precision=lax.Precision.HIGHEST, preferred_element_type=jnp.float32
-    )
-    summed, tile = lax.psum(
-        (
-            lax.dot_general(
-                gradients,
-                pivot,
-                numbers,
-                precision=lax.Precision.HIGHEST,
-                preferred_element_type=jnp.float32,
-            ),
-            tile_term,
+
+    rows_n = lax.axis_size("rows")
+    core = lax.axis_index("rows") % 2
+    half = B // 2
+    mine = lax.dynamic_slice_in_dim(pivot, core * half, half, 0)
+    tile_half = lax.psum(
+        lax.dot_general(
+            mine, pivot, numbers, precision=lax.Precision.HIGHEST, preferred_element_type=jnp.float32
         ),
         "dims",
     )
-    column = lax.dynamic_slice_in_dim(summed, lax.axis_index("dims") * share, share, 0)
+    other_half = lax.ppermute(tile_half, "rows", [(i, i ^ 1) for i in range(rows_n)])
+    tile = jnp.where(
+        core == 0,
+        jnp.concatenate([tile_half, other_half], axis=0),
+        jnp.concatenate([other_half, tile_half], axis=0),
+    )
+
+    column = lax.psum_scatter(
+        lax.dot_general(
+            gradients,
+            pivot,
+            numbers,
+            precision=lax.Precision.HIGHEST,
+            preferred_element_type=jnp.float32,
+        ),
+        "dims",
+        scatter_dimension=0,
+        tiled=True,
+    )
     first = lax.axis_index("rows") * local_rows + lax.axis_index("dims") * share
     row_ids = first + jnp.arange(share, dtype=jnp.int32)[:, None]
     col_ids = position * B + jnp.arange(B, dtype=jnp.int32)[None, :]

time: 808 us -> 576 us (0.71)
  waiting for transfers between devices: 341 us -> 119 us
    psum x1, waiting for transfers between devices: 227 us -> 1.2 us  [per_device(): lax.psum(lax.dot_general(mine, pivot, numbers, precision=lax.Precision.HI...]
  transfers between devices with their start and end apart: 2 -> 4, of which waited for: 2 -> 3; matrix products, arithmetic and copies ran while one was open for 0% -> 66% of each run, Pallas kernels for 0% -> 0%
where the time goes in v1:
time: 576 us; the launch traced here: 570 us
  other arithmetic  267 us (46%)
  waiting for transfers between devices  119 us (21%)
  matrix products  109 us (19%)
  local copies, waits for them, and re-layouts  50.4 us (9%)
  between operations  23.5 us (4%)
    another operation x30, other arithmetic, per_device(): factor = jnp.linalg.cholesky(tile + ridge * jnp.eye(B, dtype=jnp.float32))  168 us
    psum x1, waiting for transfers between devices, broadcast(): return lax.psum(jnp.where(mine, array, jnp.zeros_like(array)), axis)  115 us
    another operation x3, other arithmetic, per_device(): lax.linalg.triangular_solve(factor, column, left_side=False, lower=True,...  83.7 us
    dot_general x1, matrix products, per_device(): lax.dot_general(gradients, pivot, numbers, precision=lax.Precision.HIGHES...  57.3 us
    another operation x14, matrix products, per_device(): factor = jnp.linalg.cholesky(tile + ridge * jnp.eye(B, dtype=jnp.float32))  25.9 us
    another operation x40, local copies, waits for them, and re-layouts  23.7 us
    another operation x15, matrix products, per_device(): lax.linalg.triangular_solve(factor, column, left_side=False, lower=True,...  16 us
  transfers between devices with their start and end apart: 4, of which 3 were waited for; matrix products, arithmetic and copies ran while one was open for 66% of the time, Pallas kernels for 0%

profile of v1, /device:TPU:1, one launch (start us, length us, event | category | flops | bytes accessed | tf_op | source)
XLA Modules:
  0.0 569.7 jit_solution(13472106828858377014)
XLA Ops:
  11.1 4.7 constant_dynamic-slice_fusion.1
  15.8 5.3 copy.33
  21.2 2.8 broadcast_select_fusion
  24.0 114.7 %all-reduce.4.cloned.1.call-done = f32[1024,1024]{0,1:T(8,128)} async-done(((f32[1024,1024]{0,1:T(8,128)}), f32[1024,1024]{0,1:T(8,128)}) %all-reduce.4.cloned.1.call-update) | async-done | bytes 4194320 | tf_op jit(solution)/shard_map/psum | solution.py:11
  138.7 10.3 %fusion.2 = f32[512,1024]{0,1:T(8,128)} fusion(f32[1024,1024]{0,1:T(8,128)} %all-reduce.4.cloned.1.call-done, s32[]{:T(128)S(6)} %select_n.56), kind=kOutput, calls=%fused_computation.10 | convolution fusion | flops 6442450944 | bytes 8388612 | tf_op jit(solution)/shard_map/dot_general | solution.py:31
  149.1 57.3 %convolution_bitcast_fusion = f32[2048,1024]{0,1:T(8,128)} fusion(f32[1024,1024]{0,1:T(8,128)} %all-reduce.4.cloned.1.call-done, f32[2048,1024]{1,0:T(8,128)} %param.4), kind=kOutput, calls=%fused_computation.3 | convolution fusion | flops 25769803776 | bytes 20971520 | tf_op jit(solution)/shard_map/dot_general | solution.py:44
  209.8 2.7 collective-permute-done
  212.5 4.8 fusion
  217.3 5.5 copy.7
  222.8 4.4 fusion.1
  229.2 11.7 %cholesky.222 = f32[128,128]{1,0:T(8,128)S(1)} custom-call(f32[128,128]{1,0:T(8,128)S(1)} %cholesky.577), custom_call_target="Cholesky" | custom-call | tf_op jit(solution)/shard_map/jit(cholesky)/cholesky | solution.py:59
  241.1 9.8 %custom-call.62 = f32[1,128,128]{1,2,0:T(8,128)S(1)} custom-call(f32[1,128,128]{2,1,0:T(8,128)S(1)} %get-tuple-element.65), custom_call_target="InvertDiagBlocksLowerTriangular" | custom-call | tf_op jit(solution)/shard_map/jit(cholesky)/cholesky | solution.py:59
  254.2 11.7 %cholesky.243 = f32[128,128]{1,0:T(8,128)S(1)} custom-call(f32[128,128]{1,0:T(8,128)S(1)} %cholesky.581), custom_call_target="Cholesky" | custom-call | tf_op jit(solution)/shard_map/jit(cholesky)/cholesky | solution.py:59
  266.3 9.8 %custom-call.63 = f32[1,128,128]{1,2,0:T(8,128)S(1)} custom-call(f32[1,128,128]{2,1,0:T(8,128)S(1)} %get-tuple-element.63), custom_call_target="InvertDiagBlocksLowerTriangular" | custom-call | tf_op jit(solution)/shard_map/jit(cholesky)/cholesky | solution.py:59
  281.6 11.7 %cholesky.466 = f32[128,128]{1,0:T(8,128)S(1)} custom-call(f32[128,128]{1,0:T(8,128)S(1)} %cholesky.586), custom_call_target="Cholesky" | custom-call | tf_op jit(solution)/shard_map/jit(cholesky)/cholesky | solution.py:59
  293.4 9.8 %custom-call.64 = f32[1,128,128]{1,2,0:T(8,128)S(1)} custom-call(f32[1,128,128]{2,1,0:T(8,128)S(1)} %get-tuple-element.61), custom_call_target="InvertDiagBlocksLowerTriangular" | custom-call | tf_op jit(solution)/shard_map/jit(cholesky)/cholesky | solution.py:59
  305.1 3.3 slice_subtract_fusion.2
  308.5 11.7 %cholesky.485 = f32[128,128]{1,0:T(8,128)S(1)} custom-call(f32[128,128]{1,0:T(8,128)S(1)} %cholesky.591), custom_call_target="Cholesky" | custom-call | tf_op jit(solution)/shard_map/jit(cholesky)/cholesky | solution.py:59
  320.3 9.8 %custom-call.65 = f32[1,128,128]{1,2,0:T(8,128)S(1)} custom-call(f32[1,128,128]{2,1,0:T(8,128)S(1)} %get-tuple-element.59), custom_call_target="InvertDiagBlocksLowerTriangular" | custom-call | tf_op jit(solution)/shard_map/jit(cholesky)/cholesky | solution.py:59
  331.9 3.1 slice_subtract_fusion.3
  335.1 12.1 %cholesky.504 = f32[128,128]{1,0:T(8,128)S(1)} custom-call(f32[128,128]{1,0:T(8,128)S(1)} %cholesky.596), custom_call_target="Cholesky" | custom-call | tf_op jit(solution)/shard_map/jit(cholesky)/cholesky | solution.py:59
  347.3 9.8 %custom-call.66 = f32[1,128,128]{1,2,0:T(8,128)S(1)} custom-call(f32[1,128,128]{2,1,0:T(8,128)S(1)} %get-tuple-element.57), custom_call_target="InvertDiagBlocksLowerTriangular" | custom-call | tf_op jit(solution)/shard_map/jit(cholesky)/cholesky | solution.py:59
  358.9 3.1 slice_subtract_fusion.4
  362.0 11.7 %cholesky.524 = f32[128,128]{1,0:T(8,128)S(1)} custom-call(f32[128,128]{1,0:T(8,128)S(1)} %cholesky.601), custom_call_target="Cholesky" | custom-call | tf_op jit(solution)/shard_map/jit(cholesky)/cholesky | solution.py:59
  373.8 9.8 %custom-call.67 = f32[1,128,128]{1,2,0:T(8,128)S(1)} custom-call(f32[1,128,128]{2,1,0:T(8,128)S(1)} %get-tuple-element.55), custom_call_target="InvertDiagBlocksLowerTriangular" | custom-call | tf_op jit(solution)/shard_map/jit(cholesky)/cholesky | solution.py:59
  385.3 2.8 slice_subtract_fusion.5
  388.1 11.7 %cholesky.544 = f32[128,128]{1,0:T(8,128)S(1)} custom-call(f32[128,128]{1,0:T(8,128)S(1)} %cholesky.606), custom_call_target="Cholesky" | custom-call | tf_op jit(solution)/shard_map/jit(cholesky)/cholesky | solution.py:59
  400.0 9.8 %custom-call.68 = f32[1,128,128]{1,2,0:T(8,128)S(1)} custom-call(f32[1,128,128]{2,1,0:T(8,128)S(1)} %get-tuple-element.53), custom_call_target="InvertDiagBlocksLowerTriangular" | custom-call | tf_op jit(solution)/shard_map/jit(cholesky)/cholesky | solution.py:59
  413.4 11.7 %cholesky.562 = f32[128,128]{1,0:T(8,128)S(1)} custom-call(f32[128,128]{1,0:T(8,128)S(1)} %slice_subtract_fusion.6), custom_call_target="Cholesky" | custom-call | tf_op jit(solution)/shard_map/jit(cholesky)/cholesky | solution.py:59
  435.5 4.9 select_select_fusion
  440.4 24.0 %while.1 = (s32[]{:T(128)}, f32[1024,1024]{0,1:T(8,128)}, s32[8,2]{0,1:T(2,128)S(1)}, f32[8,128,128]{2,1,0:T(8,128)S(1)}, s32[]{:T(128)}) while((s32[]{:T(128)}, f32[1024,1024]{0,1:T(8,128)}, s32[8,2]{0,1:T(2,128)S(1)}, f32[8,128,128]{2,1,0:T(8,128)S(1)}, s32[]{:T(128)}) %tuple.50), condition=%wide.while_cond, body=%wide.while_body.sunk | while | flops 2 | bytes 393329 | solution.py:60
  464.3 78.8 %custom-call.69 = f32[8,128,128]{1,2,0:T(8,128)S(1)} custom-call(f32[8,128,128]{2,1,0:T(8,128)S(1)} %get-tuple-element.12), custom_call_target="InvertDiagBlocksLowerTriangular" | custom-call | tf_op jit(solution)/shard_map/triangular_solve | solution.py:60
  (126 shorter events, 74.7 us)
Async XLA Ops:
  6.5 132.2 %all-reduce.4.cloned.1.call-start = ((), (), s32[]{:S(2)}) async-start(), calls=%async_computation.1 | async-start | bytes 8388608 | tf_op jit(solution)/shard_map/psum | solution.py:11
  24.0 183.6 %all-reduce.6.cloned.1.call-start = ((), (), s32[]{:S(2)}) async-start(), calls=%async_computation.3 | async-start | bytes 4194304 | tf_op jit(solution)/shard_map/psum | solution.py:30
  149.0 394.2 %reduce-scatter.2.cloned.1.call-start = ((), (), s32[]{:S(2)}) async-start(), calls=%async_computation.2 | async-start | bytes 10485760 | tf_op jit(solution)/shard_map/reduce_scatter | solution.py:43
  207.6 4.8 collective-permute-start
  227.2 2.0 copy-start.1
  277.2 2.0 copy-start
Sparse Core Ops, SparseCore 0:
  24.1 114.5 all-reduce.3
  149.1 58.4 all-reduce.5
  210.1 80.5 reduce-scatter.1
